TPU v7x, 256 devices: a whole 4x4x8 slice. The times are simulated.
256 devices in a mesh: dp: 32 (over x, z), own: 8 (over y, core).
Axes of the slice: x: 4, y: 4, z: 8, core: 2. Of those that a mesh axis runs over, the one named last changes fastest.
Arguments:
- partials: bfloat16 [32, 64, 256, 1024], P('dp', None, None, 'own')
- owner: int32 [64, 1], replicated, may hold values from 0 to 31; in each aligned block of 64 rows (0 to 63, 64 to 127, ...) at most 4 rows name the same one
- momentum: float32 [32, 4, 256, 1024], P('dp', None, None, 'own'), may hold values from -1.2 to 1.2
- master: float32 [32, 4, 256, 1024], P('dp', None, None, 'own'), may hold values from -0.3 to 0.3
Outputs:
- new_momentum: float32 [32, 4, 256, 1024], P('dp', None, None, 'own')
- new_master: float32 [32, 4, 256, 1024], P('dp', None, None, 'own')
- new_weights: bfloat16 [64, 256, 1024], P(None, None, 'own')
Inputs may be any that keep to these rules, and one draw needn't show every extreme that they name: `owner`: every group owns at least one block and at most 4 blocks; some group owns exactly 4.
All inputs are finite; a program needn't handle non-finite values.
Results may differ from a plain program's by a relative error of at most 0.0007.
Values may be sent and summed in bfloat16 or wider, within the bound.
No kernel may reach another device: no remote copies, remote signals or barrier semaphores. Data moves between devices by JAX's collectives and lax.ppermute only.
A program may use at most 128 MiB of HBM per device.

v0:
```python
import math
import jax
import jax.numpy as jnp
from jax import lax
from jax.sharding import PartitionSpec as P

D = 1024
ITERS = 5
COEF_A = 3.4445
COEF_B = -4.775
COEF_C = 2.0315
BETA = 0.95
STEP_SIZE = 0.2
DECAY = 0.1
EPSILON = 1e-07


def slot_targets(owner_list, group_count, slot_count):
    onehot = (owner_list[:, None] == jnp.arange(group_count, dtype=jnp.int32)[None, :]).astype(
        jnp.int32
    )
    before = jnp.cumsum(onehot, axis=0) - onehot
    ranks = jnp.sum(before * onehot, axis=1)
    return owner_list * slot_count + ranks


def slot_sources(target, slot_count, block_count):
    positions = jnp.arange(slot_count, dtype=jnp.int32)
    matches = positions[:, None] == target[None, :]
    present = jnp.any(matches, axis=1)
    source = jnp.sum(
        jnp.where(matches, jnp.arange(block_count, dtype=jnp.int32)[None, :], 0), axis=1
    )
    return (present, source)


def local_gram(values):
    return jnp.einsum(
        "srk,stk->srt",
        values,
        values,
        precision=lax.Precision.HIGHEST,
        preferred_element_type=jnp.float32,
    )


def gram_total(values):
    return lax.psum(local_gram(values), "own")


def matmul(left, right):
    return jnp.einsum(
        "srt,stu->sru",
        left,
        right,
        precision=lax.Precision.HIGHEST,
        preferred_element_type=jnp.float32,
    )


def newton_turn(ortho, gram, eye, next_gram):
    square = matmul(gram, gram)
    poly = COEF_B * gram + COEF_C * square
    product = jnp.einsum(
        "srt,stk->srk",
        poly,
        ortho,
        precision=lax.Precision.HIGHEST,
        preferred_element_type=jnp.float32,
    )
    ortho = COEF_A * ortho + product
    if next_gram:
        step = COEF_A * eye + poly
        gram = matmul(step, matmul(gram, step))
    return (ortho, gram)


def on_device(partials, owner, momentum, master):
    group_count = lax.axis_size("dp")
    local_rows = partials[0]
    block_count = local_rows.shape[0]
    slot_count = momentum.shape[1]
    block_rows = momentum.shape[2]
    owner_list = owner[:, 0]
    target = slot_targets(owner_list, group_count, slot_count)
    present, source = slot_sources(target, group_count * slot_count, block_count)
    outgoing = jnp.where(
        present[:, None, None], jnp.take(local_rows, source, axis=0).astype(jnp.float32), 0.0
    )
    gradient = lax.psum_scatter(outgoing, "dp", scatter_dimension=0, tiled=True)
    momentum_new = BETA * momentum[0] + gradient
    update = gradient + BETA * momentum_new
    update_gram = gram_total(update)
    squares = jnp.trace(update_gram, axis1=1, axis2=2)
    factor = 1.0 / (jnp.sqrt(squares) + EPSILON)
    ortho = update * factor[:, None, None]
    gram = update_gram * (factor * factor)[:, None, None]
    eye = jnp.eye(block_rows, dtype=jnp.float32)[None]
    for iteration in range(ITERS):
        ortho, gram = newton_turn(ortho, gram, eye, iteration < ITERS - 1)
    step_factor = STEP_SIZE * 0.2 * math.sqrt(max(block_rows, D))
    master_new = master[0] * (1.0 - STEP_SIZE * DECAY) - step_factor * ortho
    weights_low = master_new.astype(jnp.bfloat16)
    every_slot = lax.all_gather(weights_low, "dp", axis=0, tiled=True)
    weights = jnp.take(every_slot, target, axis=0)
    return (momentum_new[None], master_new[None], weights)


def solution(mesh):
    in_specs = (
        P("dp", None, None, "own"),
        P(),
        P("dp", None, None, "own"),
        P("dp", None, None, "own"),
    )
    out_specs = (P("dp", None, None, "own"), P("dp", None, None, "own"), P(None, None, "own"))
    return jax.shard_map(
        on_device, mesh=mesh, in_specs=in_specs, out_specs=out_specs, check_vma=False
    )
```

profile of v0, /device:TPU:1, one launch (start us, length us, event | category | flops | bytes accessed | tf_op | source)
XLA Modules:
  0.0 493.5 jit_solution(1865720809806670317)
XLA Ops:
  7.2 0.0 reduce-scatter.2.cloned.1.call-start
  7.2 0.7 fusion.39
  7.9 0.1 reduce_window_sum.11
  8.0 0.8 select_reduce_fusion.2
  8.9 0.7 multiply_add_fusion.3
  9.5 0.1 select_reduce_fusion.1
  9.7 0.1 fusion.40
  9.8 8.6 %gather_fusion = bf16[128,256,128]{2,1,0:T(8,128)(2,1)} fusion(bf16[64,256,128]{2,1,0:T(8,128)(2,1)} %bitcast.57, s32[1024]{0:T(1024)S(1)} %pad_clamp_fusion.1), kind=kCustom, calls=%fused_computation | custom fusion | bytes 16777728 | tf_op jit(solution)/shard_map/jit(_take)/gather | solution.py:88
  18.4 13.4 %convert_select_fusion = f32[128,256,128]{2,1,0:T(8,128)} fusion(bf16[128,256,128]{2,1,0:T(8,128)(2,1)} %gather_fusion, pred[128]{0:T(512)(128)(4,1)S(1)} %compare_and_fusion, pred[128]{0:T(512)(128)(4,1)S(1)} %fusion.40), kind=kLoop, calls=%fused_computation.2 | loop fusion | flops 12582912 | bytes 25166080 | tf_op jit(solution)/shard_map/jit(_where)/select_n | solution.py:87
  31.7 0.0 copy-start
  31.7 0.0 reduce-scatter.2.cloned.1.call-update
  31.8 0.0 all-reduce.2.cloned.1.call-start
  31.8 245.8 %reduce-scatter.2.cloned.1.call-done = f32[4,256,128]{2,1,0:T(8,128)} async-done(((f32[128,256,128]{2,1,0:T(8,128)}), f32[4,256,128]{2,1,0:T(8,128)}) %reduce-scatter.2.cloned.1.call-update) | async-done | bytes 524304 | tf_op jit(solution)/shard_map/reduce_scatter | solution.py:90
  277.7 0.0 copy-done
  277.7 3.3 fusion.38
  280.9 0.0 all-reduce.2.cloned.1.call-update
  281.0 0.2 all-gather.2.cloned.1.call-start
  281.2 0.0 copy-start.1
  281.3 68.5 %all-reduce.2.cloned.1.call-done = f32[4,256,256]{2,1,0:T(8,128)} async-done(((f32[4,256,256]{2,1,0:T(8,128)}), f32[4,256,256]{2,1,0:T(8,128)}) %all-reduce.2.cloned.1.call-update) | async-done | bytes 1048592 | tf_op jit(solution)/shard_map/psum | solution.py:48
  349.7 1.4 select_reduce_fusion
  351.2 3.4 fusion.4
  354.6 2.5 fusion.21
  357.1 1.2 fusion.19
  358.3 1.3 fusion.3
  359.6 1.2 fusion.17
  360.8 0.0 copy-done.1
  360.8 1.2 convolution_add_fusion.4
  362.0 1.1 convolution_add_fusion.3
  363.0 1.2 fusion.15
  364.2 1.3 fusion.2
  365.5 1.4 fusion.13
  366.9 1.1 convolution_add_fusion.2
  368.0 1.2 fusion.11
  369.2 0.0 copy-start.2
  369.2 1.3 fusion.1
  370.5 0.0 copy-start.3
  370.5 1.2 fusion.9
  371.7 1.1 convolution_add_fusion.1
  372.8 1.2 fusion.7
  374.0 1.3 fusion
  375.3 0.0 copy-done.2
  375.3 2.0 fusion.45
  377.3 0.0 all-gather.2.cloned.1.call-update
  377.3 0.0 copy-done.3
  377.3 0.9 fusion.36
  378.2 97.7 %all-gather.2.cloned.1.call-done = bf16[128,256,128]{2,1,0:T(8,128)(2,1)} async-done(((bf16[4,256,128]{2,1,0:T(8,128)(2,1)}), bf16[128,256,128]{2,1,0:T(8,128)(2,1)}) %all-gather.2.cloned.1.call-update) | async-done | bytes 8388624 | tf_op jit(solution)/shard_map/all_gather | solution.py:104
  475.9 6.5 %gather_fusion.1 = bf16[64,256,128]{2,1,0:T(8,128)(2,1)} fusion(bf16[128,256,128]{2,1,0:T(8,128)(2,1)} %all-gather.2.cloned.1.call-done, s32[1024]{0:T(1024)S(1)} %pad_clamp_fusion), kind=kCustom, calls=%fused_computation.1 | custom fusion | bytes 8388864 | tf_op jit(solution)/shard_map/jit(_take)/gather | solution.py:105
  482.4 4.6 broadcast_select_fusion
  (8 shorter events, 0.1 us)
Async XLA Ops:
  7.2 270.5 %reduce-scatter.2.cloned.1.call-start = ((), (), s32[]{:S(2)}) async-start(), calls=%async_computation.1 | async-start | bytes 17301504 | tf_op jit(solution)/shard_map/reduce_scatter | solution.py:90
  31.7 245.9 %copy-start = (f32[1,4,256,128]{3,2,1,0:T(8,128)S(1)}, f32[1,4,256,128]{3,2,1,0:T(8,128)}, u32[]{:S(2)}) copy-start(f32[1,4,256,128]{3,2,1,0:T(8,128)} %param.6) | copy-start | bytes 1572868
  31.8 318.0 %all-reduce.2.cloned.1.call-start = ((), (), s32[]{:S(2)}) async-start(), calls=%async_computation.2 | async-start | bytes 2097152 | tf_op jit(solution)/shard_map/psum | solution.py:48
  281.0 194.9 %all-gather.2.cloned.1.call-start = ((), (), s32[]{:S(2)}) async-start(), calls=%async_computation.3 | async-start | bytes 8650752 | tf_op jit(solution)/shard_map/all_gather | solution.py:104
  281.2 79.5 %copy-start.1 = (f32[4,256,128]{2,1,0:T(8,128)S(1)}, f32[4,256,128]{2,1,0:T(8,128)}, u32[]{:S(2)}) copy-start(f32[4,256,128]{2,1,0:T(8,128)} %reduce-scatter.2.cloned.1.call-done) | copy-start | bytes 1572868
  369.2 6.1 %copy-start.2 = (f32[1,4,256,128]{3,2,1,0:T(8,128)S(1)}, f32[1,4,256,128]{3,2,1,0:T(8,128)}, u32[]{:S(2)}) copy-start(f32[1,4,256,128]{3,2,1,0:T(8,128)} %param.7) | copy-start | bytes 1572868
  370.5 6.8 %copy-start.3 = (s32[64,1]{0,1:T(1,128)S(1)}, s32[64,1]{0,1:T(1,128)}, u32[]{:S(2)}) copy-start(s32[64,1]{0,1:T(1,128)} %param.5) | copy-start | bytes 772
Sparse Core Ops, SparseCore 0:
  31.9 245.7 reduce-scatter.1
  281.1 68.5 all-reduce.1
  377.4 98.4 all-gather.1
where the time goes:
time: 494 us
  waiting for transfers between devices  412 us (83%)
  matrix products  29.2 us (6%)
  other arithmetic  22.9 us (5%)
  local copies, waits for them, and re-layouts  15.1 us (3%)
  between operations  14 us (3%)
    reduce_scatter x1, waiting for transfers between devices, on_device(): gradient = lax.psum_scatter(outgoing, 'dp', scatter_dimension=0, tiled=True)  246 us
    all_gather x1, waiting for transfers between devices, on_device(): every_slot = lax.all_gather(weights_low, 'dp', axis=0, tiled=True)  97.7 us
    psum x1, waiting for transfers between devices, gram_total(): return lax.psum(local_gram(values), 'own')  68.5 us
    dot_general x13, matrix products, matmul(): jnp.einsum('srt,stu->sru', left, right, precision=lax.Precision.HIGHEST,...  19.5 us
    select_n x1, other arithmetic, on_device(): jnp.where(present[:, None, None], jnp.take(local_rows, source, axis=0).as...  13.4 us
  transfers between devices with their start and end apart: 3, of which 3 were waited for; matrix products, arithmetic and copies ran while one was open for 0% of the time, Pallas kernels for 0%

commit v1 on v0

--- a/solution.py
+++ b/solution.py
@@ -101,7 +101,8 @@
     step_factor = STEP_SIZE * 0.2 * math.sqrt(max(block_rows, D))
     master_new = master[0] * (1.0 - STEP_SIZE * DECAY) - step_factor * ortho
     weights_low = master_new.astype(jnp.bfloat16)
-    every_slot = lax.all_gather(weights_low, "dp", axis=0, tiled=True)
+    stack = jnp.stack([weights_low] * lax.axis_size("dp"))
+    every_slot = jnp.concatenate(lax.all_to_all(stack, "dp", 0, 0), axis=0)
     weights = jnp.take(every_slot, target, axis=0)
     return (momentum_new[None], master_new[None], weights)
 

time: 494 us -> 613 us (1.24)
  the two profiles are of different devices: /device:TPU:1 before, /device:TPU:123 now
where the time goes in v1:
time: 613 us
  waiting for transfers between devices  516 us (84%)
  matrix products  29.1 us (5%)
  other arithmetic  22.9 us (4%)
  local copies, waits for them, and re-layouts  20.4 us (3%)
  between operations  14.3 us (2%)
  starting transfers between devices  9.75 us (2%)
    reduce_scatter x1, waiting for transfers between devices, on_device(): gradient = lax.psum_scatter(outgoing, 'dp', scatter_dimension=0, tiled=True)  242 us
    all_to_all x1, waiting for transfers between devices, on_device(): every_slot = jnp.concatenate(lax.all_to_all(stack, 'dp', 0, 0), axis=0)  203 us
    psum x1, waiting for transfers between devices, gram_total(): return lax.psum(local_gram(values), 'own')  71.2 us
    dot_general x13, matrix products, matmul(): jnp.einsum('srt,stu->sru', left, right, precision=lax.Precision.HIGHEST,...  19.5 us
    select_n x1, other arithmetic, on_device(): jnp.where(present[:, None, None], jnp.take(local_rows, source, axis=0).as...  13.4 us
  transfers between devices with their start and end apart: 3, of which 3 were waited for; matrix products, arithmetic and copies ran while one was open for 0% of the time, Pallas kernels for 0%

profile of v1, /device:TPU:123, one launch (start us, length us, event | category | flops | bytes accessed | tf_op | source)
XLA Modules:
  0.0 612.6 jit_solution(17633158714084922669)
XLA Ops:
  7.2 0.0 reduce-scatter.2.cloned.1.call-start
  7.2 0.7 fusion.39
  7.9 0.1 reduce_window_sum.11
  8.0 0.8 select_reduce_fusion.2
  8.9 0.7 multiply_add_fusion.3
  9.5 0.1 select_reduce_fusion.1
  9.7 0.1 fusion.40
  9.8 8.6 %gather_fusion = bf16[128,256,128]{2,1,0:T(8,128)(2,1)} fusion(bf16[64,256,128]{2,1,0:T(8,128)(2,1)} %bitcast.58, s32[1024]{0:T(1024)S(1)} %pad_clamp_fusion.1), kind=kCustom, calls=%fused_computation | custom fusion | bytes 16777728 | tf_op jit(solution)/shard_map/jit(_take)/gather | solution.py:88
  18.4 13.4 %convert_select_fusion = f32[128,256,128]{2,1,0:T(8,128)} fusion(bf16[128,256,128]{2,1,0:T(8,128)(2,1)} %gather_fusion, pred[128]{0:T(512)(128)(4,1)S(1)} %compare_and_fusion, pred[128]{0:T(512)(128)(4,1)S(1)} %fusion.40), kind=kLoop, calls=%fused_computation.2 | loop fusion | flops 12582912 | bytes 25166080 | tf_op jit(solution)/shard_map/jit(_where)/select_n | solution.py:87
  31.7 0.0 copy-start
  31.7 0.0 reduce-scatter.2.cloned.1.call-update
  31.8 0.2 all-reduce.2.cloned.1.call-start
  32.0 241.8 %reduce-scatter.2.cloned.1.call-done = f32[4,256,128]{2,1,0:T(8,128)} async-done(((f32[128,256,128]{2,1,0:T(8,128)}), f32[4,256,128]{2,1,0:T(8,128)}) %reduce-scatter.2.cloned.1.call-update) | async-done | bytes 524304 | tf_op jit(solution)/shard_map/reduce_scatter | solution.py:90
  273.8 0.0 copy-done
  273.8 3.3 fusion.38
  277.1 0.0 all-reduce.2.cloned.1.call-update
  277.1 0.0 copy-start.1
  277.2 71.2 %all-reduce.2.cloned.1.call-done = f32[4,256,256]{2,1,0:T(8,128)} async-done(((f32[4,256,256]{2,1,0:T(8,128)}), f32[4,256,256]{2,1,0:T(8,128)}) %all-reduce.2.cloned.1.call-update) | async-done | bytes 1048592 | tf_op jit(solution)/shard_map/psum | solution.py:48
  348.4 1.4 select_reduce_fusion
  349.8 3.4 fusion.4
  353.3 2.5 fusion.21
  355.7 1.2 fusion.19
  356.9 1.3 fusion.3
  358.2 1.2 fusion.17
  359.4 0.0 copy-done.1
  359.4 1.2 convolution_add_fusion.4
  360.6 1.1 convolution_add_fusion.3
  361.7 1.2 fusion.15
  362.9 1.5 fusion.2
  364.4 1.2 fusion.13
  365.6 1.1 convolution_add_fusion.2
  366.7 1.2 fusion.11
  367.9 0.0 copy-start.2
  367.9 1.3 fusion.1
  369.2 1.2 fusion.9
  370.4 1.1 convolution_add_fusion.1
  371.4 1.2 fusion.7
  372.6 1.3 fusion
  373.9 0.0 copy-done.2
  373.9 1.9 fusion.45
  375.8 5.3 stack.2
  381.1 0.0 copy-start.3
  381.1 9.5 %all-to-all-start = ((bf16[32,4,256,128]{3,2,1,0:T(8,128)(2,1)}), bf16[32,4,256,128]{3,2,1,0:T(8,128)(2,1)}, u32[]{:S(2)}, u32[]{:S(2)}) async-start(bf16[32,4,256,128]{3,2,1,0:T(8,128)(2,1)} %stack.2), calls=%async_computation.1 | async-start | bytes 16777216 | tf_op jit(solution)/shard_map/all_to_all | solution.py:105
  390.6 0.0 copy-done.3
  390.7 0.9 fusion.36
  391.5 203.1 %all-to-all-done = bf16[32,4,256,128]{3,2,1,0:T(8,128)(2,1)} async-done(((bf16[32,4,256,128]{3,2,1,0:T(8,128)(2,1)}), bf16[32,4,256,128]{3,2,1,0:T(8,128)(2,1)}, u32[]{:S(2)}, u32[]{:S(2)}) %all-to-all-start) | async-done | bytes 8388640 | tf_op jit(solution)/shard_map/all_to_all | solution.py:105
  594.6 6.5 %gather_fusion.1 = bf16[64,256,128]{2,1,0:T(8,128)(2,1)} fusion(bf16[128,256,128]{2,1,0:T(8,128)(2,1)} %bitcast.10, s32[1024]{0:T(1024)S(1)} %pad_clamp_fusion), kind=kCustom, calls=%fused_computation.1 | custom fusion | bytes 8388864 | tf_op jit(solution)/shard_map/jit(_take)/gather | solution.py:106
  601.1 4.6 broadcast_select_fusion
  (8 shorter events, 0.1 us)
Async XLA Ops:
  7.2 266.6 %reduce-scatter.2.cloned.1.call-start = ((), (), s32[]{:S(2)}) async-start(), calls=%async_computation.2 | async-start | bytes 17301504 | tf_op jit(solution)/shard_map/reduce_scatter | solution.py:90
  31.7 242.1 %copy-start = (f32[1,4,256,128]{3,2,1,0:T(8,128)S(1)}, f32[1,4,256,128]{3,2,1,0:T(8,128)}, u32[]{:S(2)}) copy-start(f32[1,4,256,128]{3,2,1,0:T(8,128)} %param.6) | copy-start | bytes 1572868
  31.8 316.6 %all-reduce.2.cloned.1.call-start = ((), (), s32[]{:S(2)}) async-start(), calls=%async_computation.3 | async-start | bytes 2097152 | tf_op jit(solution)/shard_map/psum | solution.py:48
  277.1 82.3 %copy-start.1 = (f32[4,256,128]{2,1,0:T(8,128)S(1)}, f32[4,256,128]{2,1,0:T(8,128)}, u32[]{:S(2)}) copy-start(f32[4,256,128]{2,1,0:T(8,128)} %reduce-scatter.2.cloned.1.call-done) | copy-start | bytes 1572868
  367.9 6.0 copy-start.2
  381.1 9.5 %copy-start.3 = (s32[64,1]{0,1:T(1,128)S(1)}, s32[64,1]{0,1:T(1,128)}, u32[]{:S(2)}) copy-start(s32[64,1]{0,1:T(1,128)} %param.5) | copy-start | bytes 772
  381.1 213.5 %all-to-all-start = ((bf16[32,4,256,128]{3,2,1,0:T(8,128)(2,1)}), bf16[32,4,256,128]{3,2,1,0:T(8,128)(2,1)}, u32[]{:S(2)}, u32[]{:S(2)}) async-start(bf16[32,4,256,128]{3,2,1,0:T(8,128)(2,1)} %stack.2), calls=%async_computation.1 | async-start | bytes 16777216 | tf_op jit(solution)/shard_map/all_to_all | solution.py:105
Sparse Core Ops, SparseCore 0:
  31.9 241.8 reduce-scatter.1
  277.2 71.1 all-reduce.1

commit v2 on v0

--- a/solution.py
+++ b/solution.py
@@ -13,6 +13,7 @@
 STEP_SIZE = 0.2
 DECAY = 0.1
 EPSILON = 1e-07
+boxes_arrange = lambda u_in: jax.lax.all_gather(u_in, "own").sum(axis=0)
 
 
 def slot_targets(owner_list, group_count, slot_count):
@@ -45,7 +46,7 @@
 
 
 def gram_total(values):
-    return lax.psum(local_gram(values), "own")
+    return boxes_arrange(local_gram(values))
 
 
 def matmul(left, right):

time: 494 us -> 479 us (0.970)
  waiting for transfers between devices: 412 us -> 397 us
    psum x1 -> x0, waiting for transfers between devices: 68.5 us -> none  [gram_total(): return lax.psum(local_gram(values), 'own')]
    all_gather x0 -> x1, waiting for transfers between devices: none -> 55.3 us  [boxes_arrange = lambda u_in: jax.lax.all_gather(u_in, 'own').sum(axis=0)]
where the time goes in v2:
time: 479 us; the launch traced here: 478 us
  waiting for transfers between devices  397 us (83%)
  matrix products  25.9 us (5%)
  other arithmetic  25.8 us (5%)
  local copies, waits for them, and re-layouts  15.1 us (3%)
  between operations  14 us (3%)
    reduce_scatter x1, waiting for transfers between devices, on_device(): gradient = lax.psum_scatter(outgoing, 'dp', scatter_dimension=0, tiled=True)  246 us
    all_gather x1, waiting for transfers between devices, on_device(): every_slot = lax.all_gather(weights_low, 'dp', axis=0, tiled=True)  96.1 us
    all_gather x1, waiting for transfers between devices, boxes_arrange = lambda u_in: jax.lax.all_gather(u_in, 'own').sum(axis=0)  55.3 us
    dot_general x13, matrix products, matmul(): jnp.einsum('srt,stu->sru', left, right, precision=lax.Precision.HIGHEST,...  16.3 us
    select_n x1, other arithmetic, on_device(): jnp.where(present[:, None, None], jnp.take(local_rows, source, axis=0).as...  13.4 us
  transfers between devices with their start and end apart: 3, of which 3 were waited for; matrix products, arithmetic and copies ran while one was open for 0% of the time, Pallas kernels for 0%

profile of v2, /device:TPU:1, one launch (start us, length us, event | category | flops | bytes accessed | tf_op | source)
XLA Modules:
  0.0 478.4 jit_solution(17182615396338760026)
XLA Ops:
  7.2 0.0 reduce-scatter.2.cloned.1.call-start
  7.2 0.7 fusion.39
  7.9 0.1 reduce_window_sum.11
  8.0 0.8 select_reduce_fusion.2
  8.9 0.7 multiply_add_fusion.3
  9.5 0.1 select_reduce_fusion.1
  9.7 0.1 fusion.40
  9.8 8.6 %gather_fusion = bf16[128,256,128]{2,1,0:T(8,128)(2,1)} fusion(bf16[64,256,128]{2,1,0:T(8,128)(2,1)} %bitcast.58, s32[1024]{0:T(1024)S(1)} %pad_clamp_fusion.1), kind=kCustom, calls=%fused_computation | custom fusion | bytes 16777728 | tf_op jit(solution)/shard_map/jit(_take)/gather | solution.py:89
  18.4 13.4 %convert_select_fusion = f32[128,256,128]{2,1,0:T(8,128)} fusion(bf16[128,256,128]{2,1,0:T(8,128)(2,1)} %gather_fusion, pred[128]{0:T(512)(128)(4,1)S(1)} %compare_and_fusion, pred[128]{0:T(512)(128)(4,1)S(1)} %fusion.40), kind=kLoop, calls=%fused_computation.2 | loop fusion | flops 12582912 | bytes 25166080 | tf_op jit(solution)/shard_map/jit(_where)/select_n | solution.py:88
  31.7 0.0 copy-start
  31.7 0.0 reduce-scatter.2.cloned.1.call-update
  31.8 0.0 all-gather.6.cloned.1.call-start
  31.8 245.8 %reduce-scatter.2.cloned.1.call-done = f32[4,256,128]{2,1,0:T(8,128)} async-done(((f32[128,256,128]{2,1,0:T(8,128)}), f32[4,256,128]{2,1,0:T(8,128)}) %reduce-scatter.2.cloned.1.call-update) | async-done | bytes 524304 | tf_op jit(solution)/shard_map/reduce_scatter | solution.py:91
  277.7 0.0 copy-done
  277.7 3.3 fusion.38
  280.9 0.0 all-gather.6.cloned.1.call-update
  281.0 0.2 all-gather.4.cloned.1.call-start
  281.3 55.3 %all-gather.6.cloned.1.call-done = f32[32,256,256]{2,1,0:T(8,128)} async-done(((f32[4,256,256]{2,1,0:T(8,128)}), f32[32,256,256]{2,1,0:T(8,128)}) %all-gather.6.cloned.1.call-update) | async-done | bytes 8388624 | tf_op jit(solution)/shard_map/all_gather | solution.py:16
  336.6 4.1 reduce_sum.44
  340.6 0.0 copy-start.1
  340.6 0.2 select_reduce_fusion
  340.9 1.4 fusion.4
  342.3 1.2 fusion.21
  343.5 1.2 fusion.19
  344.7 1.3 fusion.3
  346.0 1.2 fusion.17
  347.2 0.0 copy-done.1
  347.2 1.2 convolution_add_fusion.4
  348.4 1.1 convolution_add_fusion.3
  349.5 1.2 fusion.15
  350.7 1.3 fusion.2
  352.0 1.4 fusion.13
  353.4 1.1 convolution_add_fusion.2
  354.5 1.2 fusion.11
  355.6 0.0 copy-start.2
  355.7 1.3 fusion.1
  356.9 0.0 copy-start.3
  357.0 1.2 fusion.9
  358.1 1.1 convolution_add_fusion.1
  359.2 1.2 fusion.7
  360.4 1.3 fusion
  361.7 0.0 copy-done.2
  361.7 2.0 fusion.45
  363.7 0.0 all-gather.4.cloned.1.call-update
  363.7 0.0 copy-done.3
  363.8 0.9 fusion.36
  364.6 96.1 %all-gather.4.cloned.1.call-done = bf16[128,256,128]{2,1,0:T(8,128)(2,1)} async-done(((bf16[4,256,128]{2,1,0:T(8,128)(2,1)}), bf16[128,256,128]{2,1,0:T(8,128)(2,1)}) %all-gather.4.cloned.1.call-update) | async-done | bytes 8388624 | tf_op jit(solution)/shard_map/all_gather | solution.py:105
  460.7 6.5 %gather_fusion.1 = bf16[64,256,128]{2,1,0:T(8,128)(2,1)} fusion(bf16[128,256,128]{2,1,0:T(8,128)(2,1)} %all-gather.4.cloned.1.call-done, s32[1024]{0:T(1024)S(1)} %pad_clamp_fusion), kind=kCustom, calls=%fused_computation.1 | custom fusion | bytes 8388864 | tf_op jit(solution)/shard_map/jit(_take)/gather | solution.py:106
  467.2 4.6 broadcast_select_fusion
  (8 shorter events, 0.1 us)
Async XLA Ops:
  7.2 270.5 %reduce-scatter.2.cloned.1.call-start = ((), (), s32[]{:S(2)}) async-start(), calls=%async_computation.1 | async-start | bytes 17301504 | tf_op jit(solution)/shard_map/reduce_scatter | solution.py:91
  31.7 245.9 %copy-start = (f32[1,4,256,128]{3,2,1,0:T(8,128)S(1)}, f32[1,4,256,128]{3,2,1,0:T(8,128)}, u32[]{:S(2)}) copy-start(f32[1,4,256,128]{3,2,1,0:T(8,128)} %param.6) | copy-start | bytes 1572868
  31.8 304.8 %all-gather.6.cloned.1.call-start = ((), (), s32[]{:S(2)}) async-start(), calls=%async_computation.3 | async-start | bytes 9437184 | tf_op jit(solution)/shard_map/all_gather | solution.py:16
  281.0 179.8 %all-gather.4.cloned.1.call-start = ((), (), s32[]{:S(2)}) async-start(), calls=%async_computation.2 | async-start | bytes 8650752 | tf_op jit(solution)/shard_map/all_gather | solution.py:105
  340.6 6.6 %copy-start.1 = (f32[4,256,128]{2,1,0:T(8,128)S(1)}, f32[4,256,128]{2,1,0:T(8,128)}, u32[]{:S(2)}) copy-start(f32[4,256,128]{2,1,0:T(8,128)} %reduce-scatter.2.cloned.1.call-done) | copy-start | bytes 1572868
  355.6 6.1 %copy-start.2 = (f32[1,4,256,128]{3,2,1,0:T(8,128)S(1)}, f32[1,4,256,128]{3,2,1,0:T(8,128)}, u32[]{:S(2)}) copy-start(f32[1,4,256,128]{3,2,1,0:T(8,128)} %param.7) | copy-start | bytes 1572868
  356.9 6.8 %copy-start.3 = (s32[64,1]{0,1:T(1,128)S(1)}, s32[64,1]{0,1:T(1,128)}, u32[]{:S(2)}) copy-start(s32[64,1]{0,1:T(1,128)} %param.5) | copy-start | bytes 772
Sparse Core Ops, SparseCore 0:
  31.9 245.7 reduce-scatter.1
  281.1 55.4 all-gather.5
  363.9 96.8 all-gather.3
